TPU v7x, 32 devices: a whole 2x2x4 slice. The times are simulated.
32 devices in a mesh: layer: 4 (over x, core), tok: 8 (over z, y).
Axes of the slice: x: 2, y: 2, z: 4, core: 2. Of those that a mesh axis runs over, the one named last changes fastest.
Arguments:
- active_codes: bfloat16 [4, 1024, 32], P('layer', 'tok'), may hold values from 0.19921875 to 3
- latent_ids: int32 [4, 1024, 32], P('layer', 'tok'), may hold values from 0 to 32767, as said below
- decoder: bfloat16 [4, 32768, 4096], P('layer', 'tok'), may hold values from -1 to 1
- carry_gain: float32 [4, 4096], P('layer'), may hold values from 0.1 to 1
- earlier_sum: bfloat16 [1024, 4096], P('tok'), may hold values from -6 to 6
- targets: bfloat16 [4, 1024, 4096], P('layer', 'tok'), may hold values from -6 to 6
Outputs:
- reconstruction: bfloat16 [4, 1024, 4096], P('layer', 'tok')
- code_grad: float32 [4, 1024, 32], P('layer', 'tok')
Inputs may be any that keep to these rules, and one draw needn't show every extreme that they name: `latent_ids`: A token's 32 ids in one layer are distinct. In each layer, the 128 tokens of one aligned block have at most 768 ids in any one range of 4096 consecutive latents, and in every layer one range holds exactly 768 ids of every block.
All inputs are finite; a program needn't handle non-finite values.
Results may differ from a plain program's by a relative error of at most 0.019.
Values may be sent and summed in bfloat16 or wider, within the bound.
No kernel may reach another device: no remote copies, remote signals or barrier semaphores. Data moves between devices by JAX's collectives and lax.ppermute only.
A program may use at most 256 MiB of HBM per device.

v0:
```python
import jax
import jax.numpy as jnp
from jax import lax
from jax.sharding import PartitionSpec as P

LANES = 128


def selectors(ids_all, range_size):
    base = lax.axis_index("tok") * range_size
    local = ids_all - base
    inside = (local >= 0) & (local < range_size)
    high = jnp.where(inside, local // LANES, -1)
    low = local % LANES
    high_hot = high[..., None] == jnp.arange(range_size // LANES, dtype=jnp.int32)
    low_hot = low[..., None] == jnp.arange(LANES, dtype=jnp.int32)
    return (high_hot, low_hot)


def exchange_codes(latent_ids, active_codes):
    owners = lax.axis_size("tok")
    top_count = latent_ids.shape[1]
    packed = jnp.concatenate(
        [
            (latent_ids // 256).astype(jnp.bfloat16),
            (latent_ids % 256).astype(jnp.bfloat16),
            active_codes,
        ],
        axis=1,
    )
    spread = jnp.broadcast_to(packed[None], (owners,) + packed.shape)
    gathered = lax.all_to_all(spread, "tok", split_axis=0, concat_axis=0, tiled=True)
    gathered = gathered.reshape(-1, 3 * top_count)
    ids_all = gathered[:, :top_count].astype(jnp.int32) * 256 + gathered[
        :, top_count : 2 * top_count
    ].astype(jnp.int32)
    codes_all = gathered[:, 2 * top_count :]
    return (ids_all, codes_all)


def layer_chain(decoded, carry_gain, earlier_sum, targets):
    gains = lax.all_gather(carry_gain[0], "layer", axis=0, tiled=False)
    targets_all = lax.all_gather(targets[0], "layer", axis=0, tiled=False)
    decoded_all = lax.all_gather(decoded.astype(jnp.bfloat16), "layer", axis=0, tiled=False)
    layers = gains.shape[0]
    me = lax.axis_index("layer")
    carried = earlier_sum.astype(jnp.float32)
    misfits = []
    recon_own = jnp.zeros_like(decoded)
    for m in range(layers):
        own = me == m
        term = jnp.where(own, decoded, decoded_all[m].astype(jnp.float32))
        carried = term + gains[m][None, :] * carried
        recon_own = jnp.where(own, carried, recon_own)
        misfits.append(carried - targets_all[m].astype(jnp.float32))
    running = misfits[layers - 1]
    grad_own = jnp.where(me == layers - 1, running, jnp.zeros_like(running))
    for m in range(layers - 2, -1, -1):
        running = misfits[m] + gains[m + 1][None, :] * running
        grad_own = jnp.where(me == m, running, grad_own)
    return (recon_own, grad_own)


def on_device(active_codes, latent_ids, decoder, carry_gain, earlier_sum, targets):
    range_size = decoder.shape[1]
    owners = lax.axis_size("tok")
    weights = decoder[0]
    ids_all, codes_all = exchange_codes(latent_ids[0], active_codes[0])
    tokens = ids_all.shape[0]
    high_hot, low_hot = selectors(ids_all, range_size)
    coded_high = jnp.where(high_hot, codes_all[..., None], jnp.zeros((), jnp.bfloat16))
    spread = jnp.einsum(
        "tkh,tkl->thl", coded_high, low_hot.astype(jnp.bfloat16), preferred_element_type=jnp.float32
    )
    spread = spread.astype(jnp.bfloat16).reshape(tokens, range_size)
    half = weights.shape[1] // 2
    w_first, w_second = (weights[:, :half], weights[:, half:])
    partial_first = jnp.dot(spread, w_first, preferred_element_type=jnp.float32).astype(
        jnp.bfloat16
    )
    decoded_first = lax.psum_scatter(partial_first, "tok", scatter_dimension=0, tiled=True)
    partial_second = jnp.dot(spread, w_second, preferred_element_type=jnp.float32).astype(
        jnp.bfloat16
    )
    received = lax.all_to_all(partial_second, "tok", split_axis=0, concat_axis=0, tiled=True)
    decoded_second = jnp.sum(
        received.reshape(owners, -1, received.shape[1]).astype(jnp.float32), axis=0
    )
    decoded = jnp.concatenate([decoded_first.astype(jnp.float32), decoded_second], axis=1)
    recon_full, grad_sum = layer_chain(decoded, carry_gain, earlier_sum, targets)
    grad_low = grad_sum.astype(jnp.bfloat16)
    segment = lax.all_gather(grad_low, "tok", axis=0, tiled=True)
    products = lax.dot_general(
        segment, weights, (((1,), (1,)), ((), ())), preferred_element_type=jnp.float32
    ).astype(jnp.bfloat16)
    products = products.reshape(tokens, range_size // LANES, LANES)
    picked_low = jnp.einsum(
        "thl,tkl->tkh", products, low_hot.astype(jnp.bfloat16), preferred_element_type=jnp.float32
    )
    partial_grad = jnp.sum(jnp.where(high_hot, picked_low, 0.0), axis=-1)
    returned = lax.all_to_all(partial_grad, "tok", split_axis=0, concat_axis=0, tiled=True)
    code_grad = jnp.sum(returned.reshape(owners, -1, returned.shape[1]), axis=0)
    return (recon_full.astype(jnp.bfloat16)[None], code_grad[None])


def solution(mesh):
    return jax.shard_map(
        on_device,
        mesh=mesh,
        in_specs=(
            P("layer", "tok", None),
            P("layer", "tok", None),
            P("layer", "tok", None),
            P("layer", None),
            P("tok", None),
            P("layer", "tok", None),
        ),
        out_specs=(P("layer", "tok", None), P("layer", "tok", None)),
        check_vma=False,
    )
```

profile of v0, /device:TPU:0, one launch (start us, length us, event | category | flops | bytes accessed | tf_op | source)
XLA Modules:
  0.0 465.8 jit_solution(1806440239437753471)
XLA Ops:
  8.0 0.7 fusion.42
  10.1 7.3 %all-to-all-start = ((bf16[8,128,96]{1,2,0:T(8,128)(2,1)}), bf16[8,128,96]{1,2,0:T(8,128)(2,1)S(1)}, u32[]{:S(2)}, u32[]{:S(2)}) async-start(bf16[8,128,96]{1,2,0:T(8,128)(2,1)} %broadcast_in_dim.35), calls=%async_computation | async-start | bytes 393216 | tf_op jit(solution)/shard_map/all_to_all | solution.py:32
  17.5 7.9 %all-to-all-done = bf16[8,128,96]{1,2,0:T(8,128)(2,1)S(1)} async-done(((bf16[8,128,96]{1,2,0:T(8,128)(2,1)}), bf16[8,128,96]{1,2,0:T(8,128)(2,1)S(1)}, u32[]{:S(2)}, u32[]{:S(2)}) %all-to-all-start) | async-done | bytes 196640 | tf_op jit(solution)/shard_map/all_to_all | solution.py:32
  26.2 9.7 %fusion.15 = bf16[1024,32,128]{2,1,0:T(8,128)(2,1)S(1)} fusion(s32[1024,32]{1,0:T(8,128)S(1)} %copy.17, s32[1024,32]{1,0:T(8,128)S(1)} %copy.15, bf16[1024,32]{1,0:T(8,128)(2,1)S(1)} %copy.16), kind=kOutput, calls=%fused_computation.19 | convolution fusion | flops 278921216 | bytes 8716288 | tf_op jit(solution)/shard_map/tkh,tkl->thl/dot_general | solution.py:72
  35.9 3.3 copy-done.6
  39.3 21.9 %fusion.20 = bf16[1024,2048]{1,0:T(8,128)(2,1)} fusion(bf16[4096,4096]{1,0:T(8,128)(2,1)} %bitcast.126, bf16[128,8,32,128]{3,2,1,0:T(8,128)(2,1)S(1)} %bitcast.128), kind=kOutput, calls=%fused_computation.22 | convolution fusion | flops 17181966336 | bytes 29360128 | tf_op jit(solution)/shard_map/dot_general | solution.py:78
  61.1 24.0 %fusion.25 = bf16[1024,2048]{1,0:T(8,128)(2,1)} fusion(bf16[4096,4096]{1,0:T(8,128)(2,1)} %bitcast.127, bf16[128,8,32,128]{3,2,1,0:T(8,128)(2,1)} %bitcast.129), kind=kOutput, calls=%fused_computation.23 | convolution fusion | flops 17181966336 | bytes 29360128 | tf_op jit(solution)/shard_map/dot_general | solution.py:82
  85.2 4.6 all-to-all-start.1
  90.4 103.3 %all-to-all-done.1 = bf16[8,128,2048]{2,1,0:T(8,128)(2,1)} async-done(((bf16[8,128,2048]{2,1,0:T(8,128)(2,1)}), bf16[8,128,2048]{2,1,0:T(8,128)(2,1)}, u32[]{:S(2)}, u32[]{:S(2)}) %all-to-all-start.1) | async-done | bytes 4194336 | tf_op jit(solution)/shard_map/all_to_all | solution.py:85
  193.6 3.4 convert_reduce_fusion
  197.1 18.2 %reduce-scatter.2.cloned.1.call-done = bf16[128,2048]{1,0:T(8,128)(2,1)} async-done(((bf16[1024,2048]{1,0:T(8,128)(2,1)}), bf16[128,2048]{1,0:T(8,128)(2,1)}) %reduce-scatter.2.cloned.1.call-update) | async-done | bytes 524304 | tf_op jit(solution)/shard_map/reduce_scatter | solution.py:81
  215.3 2.2 pad_maximum_fusion.1
  217.6 5.4 %all-gather = f32[4,1,4096]{2,1,0:T(1,128)S(1)} all-gather(f32[1,1,4096]{2,1,0:T(1,128)S(1)} %bitcast.123), channel_id=1, replica_groups=mesh['layer'=4,'tok'=8] {'layer'}, dimensions={0}, use_global_device_ids=true | all-gather | bytes 81920 | tf_op jit(solution)/shard_map/all_gather | solution.py:42
  223.0 1.2 convert_element_type.103
  224.3 27.4 %all-gather.5.cloned.1.call-done = bf16[4,128,4096]{2,1,0:T(8,128)(2,1)} async-done(((bf16[1,128,4096]{2,1,0:T(8,128)(2,1)}), bf16[4,128,4096]{2,1,0:T(8,128)(2,1)}) %all-gather.5.cloned.1.call-update) | async-done | bytes 4194320 | tf_op jit(solution)/shard_map/all_gather | solution.py:44
  251.7 5.4 %fusion.34 = bf16[128,4096]{1,0:T(8,128)(2,1)} fusion(bf16[128,4096]{1,0:T(8,128)(2,1)S(1)} %copy-done, f32[128,2048]{1,0:T(8,128)S(1)} %convert_reduce_fusion, f32[128,2048]{1,0:T(8,128)S(1)} %convert_element_type.103, bf16[4,128,4096]{2,1,0:T(8,128)(2,1)} %all-gather.7.cloned.1.call-done, f32[4096]{0:T(1024)S(1)} %bitcast.121, f32[4096]{0:T(1024)S(1)} %bitcast.117, ...), kind=kLoop, calls=%fused_computation.33 | loop fusion | flops 19398656 | bytes 12648452 | tf_op jit(solution)/shard_map/convert_element_type | solution.py:91
  257.1 125.1 %all-gather.9.cloned.1.call-done = bf16[1024,4096]{1,0:T(8,128)(2,1)} async-done(((bf16[128,4096]{1,0:T(8,128)(2,1)}), bf16[1024,4096]{1,0:T(8,128)(2,1)}) %all-gather.9.cloned.1.call-update) | async-done | bytes 8388624 | tf_op jit(solution)/shard_map/all_gather | solution.py:92
  382.2 42.6 %convert_bitcast_fusion = bf16[128,8,32,128]{3,1,2,0:T(8,128)(2,1)} fusion(bf16[1024,4096]{1,0:T(8,128)(2,1)} %all-gather.9.cloned.1.call-done, bf16[1,4096,4096]{2,1,0:T(8,128)(2,1)} %param.8), kind=kOutput, calls=%fused_computation.12 | convolution fusion | flops 34363932672 | bytes 50331648 | tf_op jit(solution)/shard_map/dot_general | solution.py:93
  424.8 9.7 %copy.24 = bf16[128,8,32,128]{3,2,1,0:T(8,128)(2,1)} copy(bf16[128,8,32,128]{3,1,2,0:T(8,128)(2,1)} %convert_bitcast_fusion) | data formatting | bytes 16777216
  434.5 10.7 %select_reduce_fusion = f32[1024,32]{1,0:T(8,128)} fusion(s32[1024,32]{1,0:T(8,128)S(1)} %copy-done.4, bf16[1024,32,128]{2,1,0:T(8,128)(2,1)} %bitcast.111, s32[1024,32]{1,0:T(8,128)S(1)} %copy-done.2), kind=kOutput, calls=%fused_computation.4 | convolution fusion | flops 275742720 | bytes 8781824 | tf_op jit(solution)/shard_map/thl,tkl->tkh/dot_general | solution.py:97
  445.2 1.9 copy.19
  447.1 3.4 all-to-all-start.2
  450.5 3.8 fusion.39
  454.3 3.5 all-to-all-done.2
  (33 shorter events, 3.6 us)
Async XLA Ops:
  10.1 15.2 %all-to-all-start = ((bf16[8,128,96]{1,2,0:T(8,128)(2,1)}), bf16[8,128,96]{1,2,0:T(8,128)(2,1)S(1)}, u32[]{:S(2)}, u32[]{:S(2)}) async-start(bf16[8,128,96]{1,2,0:T(8,128)(2,1)} %broadcast_in_dim.35), calls=%async_computation | async-start | bytes 393216 | tf_op jit(solution)/shard_map/all_to_all | solution.py:32
  17.4 197.9 %reduce-scatter.2.cloned.1.call-start = ((), (), s32[]{:S(2)}) async-start(), calls=%async_computation.4 | async-start | bytes 4718592 | tf_op jit(solution)/shard_map/reduce_scatter | solution.py:81
  25.8 10.1 %copy-start.1 = (s32[1024,32]{1,0:T(8,128)}, s32[1024,32]{1,0:T(8,128)S(1)}, u32[]{:S(2)}) copy-start(s32[1024,32]{1,0:T(8,128)S(1)} %copy.17) | copy-start | bytes 393220
  26.0 9.9 %copy-start.3 = (s32[1024,32]{1,0:T(8,128)}, s32[1024,32]{1,0:T(8,128)S(1)}, u32[]{:S(2)}) copy-start(s32[1024,32]{1,0:T(8,128)S(1)} %copy.15) | copy-start | bytes 393220
  35.9 3.3 copy-start.6
  85.2 108.5 %all-to-all-start.1 = ((bf16[8,128,2048]{2,1,0:T(8,128)(2,1)}), bf16[8,128,2048]{2,1,0:T(8,128)(2,1)}, u32[]{:S(2)}, u32[]{:S(2)}) async-start(bf16[8,128,2048]{2,1,0:T(8,128)(2,1)} %bitcast.112), calls=%async_computation.2 | async-start | bytes 8388608 | tf_op jit(solution)/shard_map/all_to_all | solution.py:85
  89.7 134.5 %all-gather.7.cloned.1.call-start = ((), (), s32[]{:S(2)}) async-start(), calls=%async_computation.6 | async-start | bytes 5242880 | tf_op jit(solution)/shard_map/all_gather | solution.py:43
  90.3 161.4 %all-gather.5.cloned.1.call-start = ((), (), s32[]{:S(2)}) async-start(), calls=%async_computation.5 | async-start | bytes 5242880 | tf_op jit(solution)/shard_map/all_gather | solution.py:44
  197.0 20.6 %copy-start.5 = (f32[1,4096]{1,0:T(1,128)S(1)}, f32[1,4096]{1,0:T(1,128)}, u32[]{:S(2)}) copy-start(f32[1,4096]{1,0:T(1,128)} %param.9) | copy-start | bytes 49156
  215.3 36.4 %copy-start = (bf16[128,4096]{1,0:T(8,128)(2,1)S(1)}, bf16[128,4096]{1,0:T(8,128)(2,1)}, u32[]{:S(2)}) copy-start(bf16[128,4096]{1,0:T(8,128)(2,1)} %param.10) | copy-start | bytes 3145732
  217.5 164.7 %all-gather.9.cloned.1.call-start = ((), (), s32[]{:S(2)}) async-start(), calls=%async_computation.7 | async-start | bytes 9437184 | tf_op jit(solution)/shard_map/all_gather | solution.py:92
  424.8 9.7 %copy-start.2 = (s32[1024,32]{1,0:T(8,128)S(1)}, s32[1024,32]{1,0:T(8,128)}, u32[]{:S(2)}) copy-start(s32[1024,32]{1,0:T(8,128)} %copy-done.1) | copy-start | bytes 393220
  424.8 9.7 %copy-start.4 = (s32[1024,32]{1,0:T(8,128)S(1)}, s32[1024,32]{1,0:T(8,128)}, u32[]{:S(2)}) copy-start(s32[1024,32]{1,0:T(8,128)} %copy-done.3) | copy-start | bytes 393220
  447.1 10.7 %all-to-all-start.2 = ((f32[8,128,32]{1,2,0:T(8,128)}), f32[8,128,32]{1,2,0:T(8,128)S(1)}, u32[]{:S(2)}, u32[]{:S(2)}) async-start(f32[8,128,32]{1,2,0:T(8,128)} %copy.19), calls=%async_computation.3 | async-start | bytes 262144 | tf_op jit(solution)/shard_map/all_to_all | solution.py:101
Sparse Core Ops, SparseCore 0:
  61.3 154.0 reduce-scatter.1
  257.3 124.9 all-gather.8
Sparse Core Ops, SparseCore 1:
  91.9 35.6 all-gather.6
  217.6 34.0 all-gather.4
where the time goes:
time: 466 us
  waiting for transfers between devices  286 us (61%)
  matrix products  109 us (23%)
  other arithmetic  18.2 us (4%)
  local copies, waits for them, and re-layouts  16.2 us (3%)
  between operations  15.7 us (3%)
  starting transfers between devices  15.4 us (3%)
  blocking collectives  5.43 us (1%)
    all_gather x1, waiting for transfers between devices, on_device(): segment = lax.all_gather(grad_low, 'tok', axis=0, tiled=True)  125 us
    all_to_all x1, waiting for transfers between devices, on_device(): lax.all_to_all(partial_second, 'tok', split_axis=0, concat_axis=0, tiled=...  103 us
    dot_general x1, matrix products, on_device(): lax.dot_general(segment, weights, (((1,), (1,)), ((), ())), preferred_ele...  42.6 us
    all_gather x1, waiting for transfers between devices, layer_chain(): lax.all_gather(decoded.astype(jnp.bfloat16), 'layer', axis=0, tiled=False)  27.4 us
    dot_general x1, matrix products, on_device(): jnp.dot(spread, w_second, preferred_element_type=jnp.float32)  24 us
    dot_general x1, matrix products, on_device(): jnp.dot(spread, w_first, preferred_element_type=jnp.float32)  21.9 us
    reduce_scatter x1, waiting for transfers between devices, on_device(): lax.psum_scatter(partial_first, 'tok', scatter_dimension=0, tiled=True)  18.2 us
    unnamed x15, local copies, waits for them, and re-layouts  13 us
  transfers between devices with their start and end apart: 7, of which 6 were waited for; matrix products, arithmetic and copies ran while one was open for 7% of the time, Pallas kernels for 0%

commit v1 on v0

--- a/solution.py
+++ b/solution.py
@@ -4,6 +4,23 @@
 from jax.sharding import PartitionSpec as P
 
 LANES = 128
+
+
+def joined_along(blocks, dim):
+    shape = list(blocks.shape[1:])
+    shape[dim] *= blocks.shape[0]
+    return jnp.moveaxis(blocks, 0, dim).reshape(shape)
+
+
+def ring_gather(value, axis, dim):
+    length = lax.axis_size(axis)
+    right = [(i, (i + 1) % length) for i in range(length)]
+    tiles = [value]
+    while len(tiles) < length:
+        tiles.append(lax.ppermute(tiles[-1], axis, right))
+    index = lax.axis_index(axis)
+    tiles = jnp.stack(tiles)[(index - jnp.arange(length)) % length]
+    return joined_along(tiles, dim)
 
 
 def selectors(ids_all, range_size):
@@ -89,7 +106,7 @@
     decoded = jnp.concatenate([decoded_first.astype(jnp.float32), decoded_second], axis=1)
     recon_full, grad_sum = layer_chain(decoded, carry_gain, earlier_sum, targets)
     grad_low = grad_sum.astype(jnp.bfloat16)
-    segment = lax.all_gather(grad_low, "tok", axis=0, tiled=True)
+    segment = ring_gather(grad_low, "tok", 0)
     products = lax.dot_general(
         segment, weights, (((1,), (1,)), ((), ())), preferred_element_type=jnp.float32
     ).astype(jnp.bfloat16)

time: 466 us -> 528 us (1.13)
  waiting for transfers between devices: 286 us -> 331 us
  local copies, waits for them, and re-layouts: 16.2 us -> 31.4 us
    ppermute x0 -> x7, waiting for transfers between devices: none -> 170 us  [ring_gather(): tiles.append(lax.ppermute(tiles[-1], axis, right))]
    all_gather x1 -> x0, waiting for transfers between devices: 125 us -> none  [on_device(): segment = lax.all_gather(grad_low, 'tok', axis=0, tiled=True)]
    gather x0 -> x1, local copies, waits for them, and re-layouts: none -> 8.06 us  [ring_gather(): tiles = jnp.stack(tiles)[(index - jnp.arange(length)) % length]]
    unnamed x15 -> x21, local copies, waits for them, and re-layouts: 13 us -> 19.1 us
    unnamed x0 -> x1, other arithmetic: none -> 5.4 us
    convert_element_type x1 -> x0, other arithmetic: 5.4 us -> none  [on_device(): grad_low = grad_sum.astype(jnp.bfloat16)]
  transfers between devices with their start and end apart: 7 -> 13, of which waited for: 6 -> 12; matrix products, arithmetic and copies ran while one was open for 7% -> 8% of each run, Pallas kernels for 0% -> 0%
where the time goes in v1:
time: 528 us; the launch traced here: 527 us
  waiting for transfers between devices  331 us (63%)
  matrix products  109 us (21%)
  local copies, waits for them, and re-layouts  31.4 us (6%)
  other arithmetic  18.2 us (3%)
  starting transfers between devices  17 us (3%)
  between operations  15.7 us (3%)
    ppermute x7, waiting for transfers between devices, ring_gather(): tiles.append(lax.ppermute(tiles[-1], axis, right))  170 us
    all_to_all x1, waiting for transfers between devices, on_device(): lax.all_to_all(partial_second, 'tok', split_axis=0, concat_axis=0, tiled=...  103 us
    dot_general x1, matrix products, on_device(): lax.dot_general(segment, weights, (((1,), (1,)), ((), ())), preferred_ele...  42.6 us
    all_gather x1, waiting for transfers between devices, layer_chain(): lax.all_gather(decoded.astype(jnp.bfloat16), 'layer', axis=0, tiled=False)  27.7 us
    dot_general x1, matrix products, on_device(): jnp.dot(spread, w_second, preferred_element_type=jnp.float32)  24 us
    dot_general x1, matrix products, on_device(): jnp.dot(spread, w_first, preferred_element_type=jnp.float32)  21.9 us
    unnamed x21, local copies, waits for them, and re-layouts  19.1 us
    reduce_scatter x1, waiting for transfers between devices, on_device(): lax.psum_scatter(partial_first, 'tok', scatter_dimension=0, tiled=True)  18.2 us
  transfers between devices with their start and end apart: 13, of which 12 were waited for; matrix products, arithmetic and copies ran while one was open for 8% of the time, Pallas kernels for 0%

profile of v1, /device:TPU:0, one launch (start us, length us, event | category | flops | bytes accessed | tf_op | source)
XLA Modules:
  0.0 527.0 jit_solution(6303029670626101970)
XLA Ops:
  10.1 7.3 %all-to-all-start = ((bf16[8,128,96]{1,2,0:T(8,128)(2,1)}), bf16[8,128,96]{1,2,0:T(8,128)(2,1)S(1)}, u32[]{:S(2)}, u32[]{:S(2)}) async-start(bf16[8,128,96]{1,2,0:T(8,128)(2,1)} %broadcast_in_dim.36), calls=%async_computation | async-start | bytes 393216 | tf_op jit(solution)/shard_map/all_to_all | solution.py:49
  17.5 7.9 %all-to-all-done = bf16[8,128,96]{1,2,0:T(8,128)(2,1)S(1)} async-done(((bf16[8,128,96]{1,2,0:T(8,128)(2,1)}), bf16[8,128,96]{1,2,0:T(8,128)(2,1)S(1)}, u32[]{:S(2)}, u32[]{:S(2)}) %all-to-all-start) | async-done | bytes 196640 | tf_op jit(solution)/shard_map/all_to_all | solution.py:49
  26.2 9.7 %fusion.15 = bf16[1024,32,128]{2,1,0:T(8,128)(2,1)S(1)} fusion(s32[1024,32]{1,0:T(8,128)S(1)} %copy.17, s32[1024,32]{1,0:T(8,128)S(1)} %copy.15, bf16[1024,32]{1,0:T(8,128)(2,1)S(1)} %copy.16), kind=kOutput, calls=%fused_computation.20 | convolution fusion | flops 278921216 | bytes 8716288 | tf_op jit(solution)/shard_map/tkh,tkl->thl/dot_general | solution.py:89
  39.2 21.9 %fusion.20 = bf16[1024,2048]{1,0:T(8,128)(2,1)} fusion(bf16[4096,4096]{1,0:T(8,128)(2,1)} %bitcast.154, bf16[128,8,32,128]{3,2,1,0:T(8,128)(2,1)S(1)} %bitcast.156), kind=kOutput, calls=%fused_computation.23 | convolution fusion | flops 17181966336 | bytes 29360128 | tf_op jit(solution)/shard_map/dot_general | solution.py:95
  61.1 24.0 %fusion.25 = bf16[1024,2048]{1,0:T(8,128)(2,1)} fusion(bf16[4096,4096]{1,0:T(8,128)(2,1)} %bitcast.155, bf16[128,8,32,128]{3,2,1,0:T(8,128)(2,1)} %bitcast.157), kind=kOutput, calls=%fused_computation.24 | convolution fusion | flops 17181966336 | bytes 29360128 | tf_op jit(solution)/shard_map/dot_general | solution.py:99
  85.0 4.6 all-to-all-start.1
  90.4 103.2 %all-to-all-done.1 = bf16[8,128,2048]{2,1,0:T(8,128)(2,1)} async-done(((bf16[8,128,2048]{2,1,0:T(8,128)(2,1)}), bf16[8,128,2048]{2,1,0:T(8,128)(2,1)}, u32[]{:S(2)}, u32[]{:S(2)}) %all-to-all-start.1) | async-done | bytes 4194336 | tf_op jit(solution)/shard_map/all_to_all | solution.py:102
  197.0 18.2 %reduce-scatter.2.cloned.1.call-done = bf16[128,2048]{1,0:T(8,128)(2,1)} async-done(((bf16[1024,2048]{1,0:T(8,128)(2,1)}), bf16[128,2048]{1,0:T(8,128)(2,1)}) %reduce-scatter.2.cloned.1.call-update) | async-done | bytes 524304 | tf_op jit(solution)/shard_map/reduce_scatter | solution.py:98
  217.4 5.2 all-gather
  223.9 27.7 %all-gather.4.cloned.1.call-done = bf16[4,128,4096]{2,1,0:T(8,128)(2,1)} async-done(((bf16[1,128,4096]{2,1,0:T(8,128)(2,1)}), bf16[4,128,4096]{2,1,0:T(8,128)(2,1)}) %all-gather.4.cloned.1.call-update) | async-done | bytes 4194320 | tf_op jit(solution)/shard_map/all_gather | solution.py:61
  251.6 5.4 %bitcast_dynamic-update-slice_fusion.7 = (bf16[8,128,4096]{2,1,0:T(8,128)(2,1)}, bf16[128,4096]{1,0:T(8,128)(2,1)S(1)}) fusion(bf16[4,128,4096]{2,1,0:T(8,128)(2,1)} %all-gather.6.cloned.1.call-done, bf16[4,128,4096]{2,1,0:T(8,128)(2,1)} %all-gather.4.cloned.1.call-done, pred[]{:T(512)S(6)} %eq.25, f32[4096]{0:T(1024)S(1)} %bitcast.143, pred[]{:T(512)S(6)} %eq.55, ...), kind=kLoop, calls=%fused_computation.61 | loop fusion | flops 19398656 | bytes 13697028
  258.5 26.5 %collective-permute-done = bf16[128,4096]{1,0:T(8,128)(2,1)S(1)} collective-permute-done((bf16[128,4096]{1,0:T(8,128)(2,1)S(1)}, bf16[128,4096]{1,0:T(8,128)(2,1)S(1)}, u32[]{:S(2)}, u32[]{:S(2)}) %collective-permute-start) | collective-permute-done | bytes 1048608 | tf_op jit(solution)/shard_map/ppermute | solution.py:20
  285.0 27.2 %collective-permute-done.1 = bf16[128,4096]{1,0:T(8,128)(2,1)S(1)} collective-permute-done((bf16[128,4096]{1,0:T(8,128)(2,1)S(1)}, bf16[128,4096]{1,0:T(8,128)(2,1)S(1)}, u32[]{:S(2)}, u32[]{:S(2)}) %collective-permute-start.1) | collective-permute-done | bytes 1048608 | tf_op jit(solution)/shard_map/ppermute | solution.py:20
  312.2 26.3 %collective-permute-done.2 = bf16[128,4096]{1,0:T(8,128)(2,1)S(1)} collective-permute-done((bf16[128,4096]{1,0:T(8,128)(2,1)S(1)}, bf16[128,4096]{1,0:T(8,128)(2,1)S(1)}, u32[]{:S(2)}, u32[]{:S(2)}) %collective-permute-start.2) | collective-permute-done | bytes 1048608 | tf_op jit(solution)/shard_map/ppermute | solution.py:20
  338.5 25.3 %collective-permute-done.3 = bf16[128,4096]{1,0:T(8,128)(2,1)S(1)} collective-permute-done((bf16[128,4096]{1,0:T(8,128)(2,1)S(1)}, bf16[128,4096]{1,0:T(8,128)(2,1)S(1)}, u32[]{:S(2)}, u32[]{:S(2)}) %collective-permute-start.3) | collective-permute-done | bytes 1048608 | tf_op jit(solution)/shard_map/ppermute | solution.py:20
  365.9 22.3 %collective-permute-done.4 = bf16[128,4096]{1,0:T(8,128)(2,1)S(1)} collective-permute-done((bf16[128,4096]{1,0:T(8,128)(2,1)S(1)}, bf16[128,4096]{1,0:T(8,128)(2,1)S(1)}, u32[]{:S(2)}, u32[]{:S(2)}) %collective-permute-start.4) | collective-permute-done | bytes 1048608 | tf_op jit(solution)/shard_map/ppermute | solution.py:20
  390.3 21.4 %collective-permute-done.5 = bf16[128,4096]{1,0:T(8,128)(2,1)S(1)} collective-permute-done((bf16[128,4096]{1,0:T(8,128)(2,1)S(1)}, bf16[128,4096]{1,0:T(8,128)(2,1)S(1)}, u32[]{:S(2)}, u32[]{:S(2)}) %collective-permute-start.5) | collective-permute-done | bytes 1048608 | tf_op jit(solution)/shard_map/ppermute | solution.py:20
  413.8 20.5 %collective-permute-done.6 = bf16[128,4096]{1,0:T(8,128)(2,1)S(1)} collective-permute-done((bf16[128,4096]{1,0:T(8,128)(2,1)S(1)}, bf16[128,4096]{1,0:T(8,128)(2,1)S(1)}, u32[]{:S(2)}, u32[]{:S(2)}) %collective-permute-start.6) | collective-permute-done | bytes 1048608 | tf_op jit(solution)/shard_map/ppermute | solution.py:20
  435.4 8.1 %gather_fusion = bf16[8,128,4096]{2,1,0:T(8,128)(2,1)} fusion(bf16[8,128,4096]{2,1,0:T(8,128)(2,1)} %bitcast_dynamic-update-slice_fusion, s32[1024]{0:T(1024)S(1)} %pad_clamp_fusion), kind=kCustom, calls=%fused_computation | custom fusion | bytes 16777248 | tf_op jit(solution)/shard_map/gather | solution.py:22
  443.5 42.6 %convert_bitcast_fusion = bf16[128,8,32,128]{3,1,2,0:T(8,128)(2,1)} fusion(bf16[1024,4096]{1,0:T(8,128)(2,1)} %bitcast.138, bf16[1,4096,4096]{2,1,0:T(8,128)(2,1)} %param.8), kind=kOutput, calls=%fused_computation.13 | convolution fusion | flops 34363932672 | bytes 50331648 | tf_op jit(solution)/shard_map/dot_general | solution.py:110
  486.1 9.5 %copy.24 = bf16[128,8,32,128]{3,2,1,0:T(8,128)(2,1)} copy(bf16[128,8,32,128]{3,1,2,0:T(8,128)(2,1)} %convert_bitcast_fusion) | data formatting | bytes 16777216
  495.7 10.7 %select_reduce_fusion = f32[1024,32]{1,0:T(8,128)} fusion(s32[1024,32]{1,0:T(8,128)S(1)} %copy-done.4, bf16[1024,32,128]{2,1,0:T(8,128)(2,1)} %bitcast.139, s32[1024,32]{1,0:T(8,128)S(1)} %copy-done.2), kind=kOutput, calls=%fused_computation.5 | convolution fusion | flops 275742720 | bytes 8781824 | tf_op jit(solution)/shard_map/thl,tkl->tkh/dot_general | solution.py:114
  511.6 3.8 fusion.39
  515.4 3.5 all-to-all-done.2
  (54 shorter events, 28.5 us)
Async XLA Ops:
  10.1 15.2 %all-to-all-start = ((bf16[8,128,96]{1,2,0:T(8,128)(2,1)}), bf16[8,128,96]{1,2,0:T(8,128)(2,1)S(1)}, u32[]{:S(2)}, u32[]{:S(2)}) async-start(bf16[8,128,96]{1,2,0:T(8,128)(2,1)} %broadcast_in_dim.36), calls=%async_computation | async-start | bytes 393216 | tf_op jit(solution)/shard_map/all_to_all | solution.py:49
  17.4 197.8 %reduce-scatter.2.cloned.1.call-start = ((), (), s32[]{:S(2)}) async-start(), calls=%async_computation.4 | async-start | bytes 4718592 | tf_op jit(solution)/shard_map/reduce_scatter | solution.py:98
  25.8 10.1 %copy-start.1 = (s32[1024,32]{1,0:T(8,128)}, s32[1024,32]{1,0:T(8,128)S(1)}, u32[]{:S(2)}) copy-start(s32[1024,32]{1,0:T(8,128)S(1)} %copy.17) | copy-start | bytes 393220
  26.0 9.9 %copy-start.3 = (s32[1024,32]{1,0:T(8,128)}, s32[1024,32]{1,0:T(8,128)S(1)}, u32[]{:S(2)}) copy-start(s32[1024,32]{1,0:T(8,128)S(1)} %copy.15) | copy-start | bytes 393220
  35.9 3.2 copy-start.6
  85.0 108.6 %all-to-all-start.1 = ((bf16[8,128,2048]{2,1,0:T(8,128)(2,1)}), bf16[8,128,2048]{2,1,0:T(8,128)(2,1)}, u32[]{:S(2)}, u32[]{:S(2)}) async-start(bf16[8,128,2048]{2,1,0:T(8,128)(2,1)} %bitcast.140), calls=%async_computation.2 | async-start | bytes 8388608 | tf_op jit(solution)/shard_map/all_to_all | solution.py:102
  89.6 134.3 %all-gather.6.cloned.1.call-start = ((), (), s32[]{:S(2)}) async-start(), calls=%async_computation.6 | async-start | bytes 5242880 | tf_op jit(solution)/shard_map/all_gather | solution.py:60
  90.2 127.2 %copy-start.5 = (f32[1,4096]{1,0:T(1,128)S(1)}, f32[1,4096]{1,0:T(1,128)}, u32[]{:S(2)}) copy-start(f32[1,4096]{1,0:T(1,128)} %param.9) | copy-start | bytes 49156
  90.2 161.4 %all-gather.4.cloned.1.call-start = ((), (), s32[]{:S(2)}) async-start(), calls=%async_computation.5 | async-start | bytes 5242880 | tf_op jit(solution)/shard_map/all_gather | solution.py:61
  197.0 54.6 %copy-start = (bf16[128,4096]{1,0:T(8,128)(2,1)S(1)}, bf16[128,4096]{1,0:T(8,128)(2,1)}, u32[]{:S(2)}) copy-start(bf16[128,4096]{1,0:T(8,128)(2,1)} %param.10) | copy-start | bytes 3145732
  257.0 28.0 %collective-permute-start = (bf16[128,4096]{1,0:T(8,128)(2,1)S(1)}, bf16[128,4096]{1,0:T(8,128)(2,1)S(1)}, u32[]{:S(2)}, u32[]{:S(2)}) collective-permute-start(bf16[128,4096]{1,0:T(8,128)(2,1)S(1)} %get-tuple-element.3), channel_id=1, source_target_pairs={{0,1},{1,2},{2,3},{3,4},{4,5},{5,6},{6,7},{7,0},{8,9},{9,10},{10,1... | collective-permute-start | bytes 3145736 | tf_op jit(solution)/shard_map/ppermute | solution.py:20
  285.0 27.2 %collective-permute-start.1 = (bf16[128,4096]{1,0:T(8,128)(2,1)S(1)}, bf16[128,4096]{1,0:T(8,128)(2,1)S(1)}, u32[]{:S(2)}, u32[]{:S(2)}) collective-permute-start(bf16[128,4096]{1,0:T(8,128)(2,1)S(1)} %collective-permute-done), channel_id=1, source_target_pairs={{0,1},{1,2},{2,3},{3,4},{4,5},{5,6},{6,7},{7,0},{8,9},{9,10},{10,1... | collective-permute-start | bytes 3145736 | tf_op jit(solution)/shard_map/ppermute | solution.py:20
  312.2 26.3 %collective-permute-start.2 = (bf16[128,4096]{1,0:T(8,128)(2,1)S(1)}, bf16[128,4096]{1,0:T(8,128)(2,1)S(1)}, u32[]{:S(2)}, u32[]{:S(2)}) collective-permute-start(bf16[128,4096]{1,0:T(8,128)(2,1)S(1)} %collective-permute-done.1), channel_id=1, source_target_pairs={{0,1},{1,2},{2,3},{3,4},{4,5},{5,6},{6,7},{7,0},{8,9},{9,10},{10,1... | collective-permute-start | bytes 3145736 | tf_op jit(solution)/shard_map/ppermute | solution.py:20
  338.5 25.3 %collective-permute-start.3 = (bf16[128,4096]{1,0:T(8,128)(2,1)S(1)}, bf16[128,4096]{1,0:T(8,128)(2,1)S(1)}, u32[]{:S(2)}, u32[]{:S(2)}) collective-permute-start(bf16[128,4096]{1,0:T(8,128)(2,1)S(1)} %collective-permute-done.2), channel_id=1, source_target_pairs={{0,1},{1,2},{2,3},{3,4},{4,5},{5,6},{6,7},{7,0},{8,9},{9,10},{10,1... | collective-permute-start | bytes 3145736 | tf_op jit(solution)/shard_map/ppermute | solution.py:20
  363.8 24.4 %collective-permute-start.4 = (bf16[128,4096]{1,0:T(8,128)(2,1)S(1)}, bf16[128,4096]{1,0:T(8,128)(2,1)S(1)}, u32[]{:S(2)}, u32[]{:S(2)}) collective-permute-start(bf16[128,4096]{1,0:T(8,128)(2,1)S(1)} %collective-permute-done.3), channel_id=1, source_target_pairs={{0,1},{1,2},{2,3},{3,4},{4,5},{5,6},{6,7},{7,0},{8,9},{9,10},{10,1... | collective-permute-start | bytes 3145736 | tf_op jit(solution)/shard_map/ppermute | solution.py:20
  388.2 23.5 %collective-permute-start.5 = (bf16[128,4096]{1,0:T(8,128)(2,1)S(1)}, bf16[128,4096]{1,0:T(8,128)(2,1)S(1)}, u32[]{:S(2)}, u32[]{:S(2)}) collective-permute-start(bf16[128,4096]{1,0:T(8,128)(2,1)S(1)} %collective-permute-done.4), channel_id=1, source_target_pairs={{0,1},{1,2},{2,3},{3,4},{4,5},{5,6},{6,7},{7,0},{8,9},{9,10},{10,1... | collective-permute-start | bytes 3145736 | tf_op jit(solution)/shard_map/ppermute | solution.py:20
  411.7 22.6 %collective-permute-start.6 = (bf16[128,4096]{1,0:T(8,128)(2,1)S(1)}, bf16[128,4096]{1,0:T(8,128)(2,1)S(1)}, u32[]{:S(2)}, u32[]{:S(2)}) collective-permute-start(bf16[128,4096]{1,0:T(8,128)(2,1)S(1)} %collective-permute-done.5), channel_id=1, source_target_pairs={{0,1},{1,2},{2,3},{3,4},{4,5},{5,6},{6,7},{7,0},{8,9},{9,10},{10,1... | collective-permute-start | bytes 3145736 | tf_op jit(solution)/shard_map/ppermute | solution.py:20
  486.1 9.6 %copy-start.2 = (s32[1024,32]{1,0:T(8,128)S(1)}, s32[1024,32]{1,0:T(8,128)}, u32[]{:S(2)}) copy-start(s32[1024,32]{1,0:T(8,128)} %copy-done.1) | copy-start | bytes 393220
  486.1 9.6 %copy-start.4 = (s32[1024,32]{1,0:T(8,128)S(1)}, s32[1024,32]{1,0:T(8,128)}, u32[]{:S(2)}) copy-start(s32[1024,32]{1,0:T(8,128)} %copy-done.3) | copy-start | bytes 393220
  508.3 10.7 %all-to-all-start.2 = ((f32[8,128,32]{1,2,0:T(8,128)}), f32[8,128,32]{1,2,0:T(8,128)S(1)}, u32[]{:S(2)}, u32[]{:S(2)}) async-start(f32[8,128,32]{1,2,0:T(8,128)} %copy.19), calls=%async_computation.3 | async-start | bytes 262144 | tf_op jit(solution)/shard_map/all_to_all | solution.py:118
Sparse Core Ops, SparseCore 0:
  61.2 154.0 reduce-scatter.1
Sparse Core Ops, SparseCore 1:
  91.7 35.6 all-gather.5
  217.5 34.1 all-gather.3
